TPU v7x, 128 devices: a whole 4x4x4 slice. The times are simulated.
128 devices in a mesh: guid: 2 (over x_hi), req: 4 (over x_lo, core), seq: 16 (over y, z).
Axes of the slice: x: 4 (x_hi: 2, x_lo: 2; x = x_hi * 2 + x_lo), y: 4, z: 4, core: 2. Of those that a mesh axis runs over, the one named last changes fastest.
Arguments:
- img_hidden: bfloat16 [2, 24, 1024, 1536], P('guid', 'req', 'seq'), may hold values from -6 to 6
- txt_hidden: bfloat16 [2, 24, 192, 1536], P('guid', 'req', 'seq'), may hold values from -6 to 6
- img_mod: float32 [2, 24, 5, 1536], P('guid', 'req')
- txt_mod: float32 [2, 24, 2, 1536], P('guid', 'req'), may hold values from -3 to 3
- w_img_qkv: bfloat16 [1536, 3072], P(('guid', 'req', 'seq')), may hold values from -0.15625 to 0.15625
- w_txt_qkv: bfloat16 [1536, 3072], P(('guid', 'req', 'seq')), may hold values from -0.15625 to 0.15625
- w_out: bfloat16 [1024, 1536], P(('guid', 'req', 'seq')), may hold values from -0.1875 to 0.1875
- w_head: bfloat16 [1536, 64], P(('guid', 'req', 'seq')), may hold values from -0.15625 to 0.15625
- text_lengths: int32 [2, 24], P('guid', 'req'), may hold values from 1 to 154, as said below
- latent: float32 [24, 1024, 64], P('req', 'seq', 'guid'), may hold values from -6 to 6
- step: int32 [1], replicated, may hold values from 0 to 27
Outputs:
- advanced: float32 [24, 1024, 64], P('req', 'seq', 'guid')
- guided: float32 [24, 1024, 64], P('req', 'seq', 'guid')
Inputs may be any that keep to these rules, and one draw needn't show every extreme that they name: `text_lengths`: in each half one prompt has 154 text tokens and another has 1.
All inputs are finite; a program needn't handle non-finite values.
Results may differ from a plain program's by a relative error of at most 0.012.
The roundings to bfloat16 on the way count: a program that leaves them out, or rounds other values in their place, can miss the bound.
Values may be sent and summed in bfloat16 or wider, within the bound.
No kernel may reach another device: no remote copies, remote signals or barrier semaphores. Data moves between devices by JAX's collectives and lax.ppermute only.
A program may use at most 192 MiB of HBM per device.

v0:
```python
import jax
import jax.numpy as jnp
from jax import lax
from jax.sharding import PartitionSpec as P

HD = 64
STEPS = 28
norm_epsilon = 1e-06
flow_shift = 3.0
guide_scale = 4.5


def partner(value, axis, bit):
    mask = 2**bit
    pairs = [(source, source ^ mask) for source in range(lax.axis_size(axis))]
    return lax.ppermute(value, axis, pairs)


def modulate(values_in, shift_vec, scale_vec):
    values_in = values_in.astype(jnp.float32)
    average = jnp.mean(values_in, axis=-1, keepdims=True)
    variance = jnp.mean((values_in - average) ** 2, axis=-1, keepdims=True)
    normed = (values_in - average) * lax.rsqrt(variance + norm_epsilon)
    return (normed * (1.0 + scale_vec[..., None, :]) + shift_vec[..., None, :]).astype(jnp.bfloat16)


def sigma_level(step_value):
    remaining = 1.0 - step_value / STEPS
    return flow_shift * remaining / (1.0 + (flow_shift - 1.0) * remaining)


def local(
    img_hidden,
    txt_hidden,
    img_mod,
    txt_mod,
    w_img_qkv,
    w_txt_qkv,
    w_out,
    w_head,
    text_lengths,
    latent,
    step,
):
    all_axes = ("guid", "req", "seq")
    prompts = img_hidden.shape[1]
    img_rows = img_hidden.shape[2]
    txt_rows = txt_hidden.shape[2]
    model_width = img_hidden.shape[3]
    nseq = lax.axis_size("seq")
    full_img = lax.all_gather(w_img_qkv, all_axes, axis=0, tiled=True)
    full_txt = lax.all_gather(w_txt_qkv, all_axes, axis=0, tiled=True)
    head_rows, head_cols = w_head.shape
    full_head = lax.all_gather(
        w_head.reshape(1, head_rows * head_cols), all_axes, axis=0, tiled=True
    ).reshape(-1, head_cols)
    full_out = lax.all_gather(w_out, all_axes, axis=0, tiled=True)
    image_in = modulate(img_hidden[0], img_mod[0, :, 0], img_mod[0, :, 1])
    text_in = modulate(txt_hidden[0], txt_mod[0, :, 0], txt_mod[0, :, 1])
    attn_width = full_img.shape[1] // 3
    head_count = attn_width // HD
    per_dev = head_count // nseq
    qkv_image = jnp.einsum(
        "prd,de->pre", image_in, full_img, preferred_element_type=jnp.float32
    ).astype(jnp.bfloat16)
    qkv_text = jnp.einsum(
        "prd,de->pre", text_in, full_txt, preferred_element_type=jnp.float32
    ).astype(jnp.bfloat16)
    img_split = qkv_image.reshape(prompts, img_rows, 3, nseq, per_dev * HD)
    img_heads = lax.all_to_all(img_split, "seq", 3, 1, tiled=True)
    txt_split = qkv_text[..., attn_width:].reshape(prompts, txt_rows, 2, nseq, per_dev * HD)
    txt_heads = lax.all_to_all(txt_split, "seq", 3, 1, tiled=True)
    all_img = img_heads.shape[1]
    all_txt = txt_heads.shape[1]
    query_heads = img_heads[:, :, 0, 0].reshape(prompts, all_img, per_dev, HD)
    key_heads = jnp.concatenate([img_heads[:, :, 1, 0], txt_heads[:, :, 0, 0]], axis=1).reshape(
        prompts, all_img + all_txt, per_dev, HD
    )
    value_heads = jnp.concatenate([img_heads[:, :, 2, 0], txt_heads[:, :, 1, 0]], axis=1).reshape(
        prompts, all_img + all_txt, per_dev, HD
    )
    lengths = text_lengths[0]
    scores = (
        jnp.einsum("pqhd,pkhd->phqk", query_heads, key_heads, preferred_element_type=jnp.float32)
        * 0.125
    )
    position = jnp.arange(all_img + all_txt, dtype=jnp.int32)
    allowed = (position < all_img)[None, :] | ((position - all_img)[None, :] < lengths[:, None])
    scores = jnp.where(allowed[:, None, None, :], scores, -1e30)
    highest = jnp.max(scores, axis=-1)
    weights = jnp.exp(scores - highest[..., None])
    totals = jnp.sum(weights, axis=-1)
    accumulated = jnp.einsum(
        "phqk,pkhd->pqhd",
        weights.astype(jnp.bfloat16),
        value_heads,
        preferred_element_type=jnp.float32,
    )
    mixture = accumulated / jnp.transpose(totals, (0, 2, 1))[..., None]
    head_out = mixture.astype(jnp.bfloat16).reshape(prompts, all_img, 1, per_dev * HD)
    token_out = lax.all_to_all(head_out, "seq", 1, 2, tiled=True)
    attended = token_out.reshape(prompts * img_rows, attn_width)
    projected = jnp.dot(attended, full_out, preferred_element_type=jnp.float32)
    residual = img_hidden[0].astype(jnp.float32) + img_mod[0, :, 2][:, None, :] * projected.reshape(
        prompts, img_rows, model_width
    )
    final_in = modulate(residual, img_mod[0, :, 3], img_mod[0, :, 4])
    guid_index = lax.axis_index("guid")
    half_width = latent.shape[2]
    own_start = guid_index * half_width
    other_start = (1 - guid_index) * half_width
    whole_velocity = jnp.einsum(
        "prd,dc->prc", final_in, full_head, preferred_element_type=jnp.float32
    )
    own_velocity = lax.dynamic_slice_in_dim(whole_velocity, own_start, half_width, 2)
    partner_part = lax.dynamic_slice_in_dim(whole_velocity, other_start, half_width, 2)
    other_velocity = partner(partner_part.astype(jnp.bfloat16), "guid", 0).astype(
        partner_part.dtype
    )
    cond_velocity = jnp.where(guid_index == 0, own_velocity, other_velocity)
    free_velocity = jnp.where(guid_index == 0, other_velocity, own_velocity)
    guided = free_velocity + guide_scale * (cond_velocity - free_velocity)
    step_value = step[0].astype(jnp.float32)
    advanced = latent + (sigma_level(step_value + 1.0) - sigma_level(step_value)) * guided
    return (advanced, guided)


def solution(mesh):
    placed = (
        P("guid", "req", "seq", None),
        P("guid", "req", "seq", None),
        P("guid", "req", None, None),
        P("guid", "req", None, None),
        P(("guid", "req", "seq"), None),
        P(("guid", "req", "seq"), None),
        P(("guid", "req", "seq"), None),
        P(("guid", "req", "seq"), None),
        P("guid", "req"),
        P("req", "seq", "guid"),
        P(),
    )
    return jax.shard_map(
        local,
        mesh=mesh,
        in_specs=placed,
        out_specs=(P("req", "seq", "guid"), P("req", "seq", "guid")),
        check_vma=False,
    )
```

profile of v0, /device:TPU:0, one launch (start us, length us, event | category | flops | bytes accessed | tf_op | source)
XLA Modules:
  0.0 415.2 jit_solution(12379703206547483496)
XLA Ops:
  14.4 72.3 %all-gather.11.cloned.1.call-done = bf16[128,12,3072]{2,1,0:T(8,128)(2,1)} async-done(((bf16[1,12,3072]{2,1,0:T(8,128)(2,1)}), bf16[128,12,3072]{2,1,0:T(8,128)(2,1)}) %all-gather.11.cloned.1.call-update) | async-done | bytes 9437200 | tf_op jit(solution)/shard_map/all_gather | solution.py:52
  86.7 13.7 %reshape.207 = bf16[1536,3072,1]{1,0,2:T(8,128)(2,1)} reshape(bf16[128,12,3072]{2,1,0:T(8,128)(2,1)} %all-gather.11.cloned.1.call-done) | data formatting | bytes 18874368
  100.4 5.4 %fusion.48 = bf16[6,12,3072]{2,1,0:T(8,128)(2,1)S(1)} fusion(bf16[1536,3072,1]{1,0,2:T(8,128)(2,1)} %reshape.207, bf16[1,6,12,1536]{3,2,1,0:T(8,128)(2,1)S(1)} %copy-done.1, f32[6,1536]{1,0:T(8,128)S(1)} %get-tuple-element.19, f32[6,1536]{1,0:T(8,128)S(1)} %get-tuple-element.20, f32[6,12]{1,0:T(8,128)S(1)} %add_rsqrt_fusion.1, ...), kind=kOutput, calls=%fused_computation.53 | convolution fusion | flops 680140800 | bytes 10175040 | tf_op jit(solution)/shard_map/prd,de->pre/dot_general | solution.py:66
  108.0 6.6 %all-to-all-start.1 = ((bf16[16,2,4608]{2,1,0:T(2,128)(2,1)}), bf16[16,2,4608]{2,1,0:T(2,128)(2,1)}, u32[]{:S(2)}, u32[]{:S(2)}) async-start(bf16[16,2,4608]{2,1,0:T(2,128)(2,1)} %reshape.213), calls=%async_computation.1 | async-start | bytes 589824 | tf_op jit(solution)/shard_map/all_to_all | solution.py:72
  114.6 47.7 %all-gather.9.cloned.1.call-done = bf16[128,12,3072]{2,1,0:T(8,128)(2,1)} async-done(((bf16[1,12,3072]{2,1,0:T(8,128)(2,1)}), bf16[128,12,3072]{2,1,0:T(8,128)(2,1)}) %all-gather.9.cloned.1.call-update) | async-done | bytes 9437200 | tf_op jit(solution)/shard_map/all_gather | solution.py:51
  162.3 13.7 %reshape.206 = bf16[1536,3072,1]{1,0,2:T(8,128)(2,1)} reshape(bf16[128,12,3072]{2,1,0:T(8,128)(2,1)} %all-gather.9.cloned.1.call-done) | data formatting | bytes 18874368
  176.0 8.2 %convolution_convert_fusion = bf16[6,64,3072]{2,1,0:T(8,128)(2,1)S(1)} fusion(bf16[1536,3072,1]{1,0,2:T(8,128)(2,1)} %reshape.206, bf16[1,6,64,1536]{3,2,1,0:T(8,128)(2,1)S(1)} %copy-done, f32[6,1536]{1,0:T(8,128)} %get-tuple-element.24, f32[6,1536]{1,0:T(8,128)} %get-tuple-element.23, f32[6,64]{1,0:T(8,128)S(1)} %add_rsqrt_fusion.2, ...), kind=kOutput, calls=%fused_computation.7 | convolution fusion | flops 3628597248 | bytes 13052928 | tf_op jit(solution)/shard_map/prd,de->pre/dot_general | solution.py:63
  184.2 4.8 %reshape.182 = bf16[6,64,3,16,64]{4,3,2,1,0:T(8,128)(2,1)} reshape(bf16[6,64,3072]{2,1,0:T(8,128)(2,1)S(1)} %convolution_convert_fusion) | data formatting | bytes 4718592 | tf_op jit(solution)/shard_map/reshape | solution.py:69
  189.0 5.7 %copy.84 = bf16[6,64,3,16,64]{4,1,2,0,3:T(8,128)(2,1)} copy(bf16[6,64,3,16,64]{4,3,2,1,0:T(8,128)(2,1)} %reshape.182) | data formatting | bytes 4718592 | tf_op jit(solution)/shard_map/reshape | solution.py:69
  194.7 7.8 %reshape.215 = bf16[16,2,36864]{2,1,0:T(2,128)(2,1)} reshape(bf16[16,6,3,64,64]{4,3,2,1,0:T(8,128)(2,1)} %bitcast.122) | data formatting | bytes 4718592
  202.6 6.7 %all-to-all-start = ((bf16[16,2,36864]{2,1,0:T(2,128)(2,1)}), bf16[16,2,36864]{2,1,0:T(2,128)(2,1)S(1)}, u32[]{:S(2)}, u32[]{:S(2)}) async-start(bf16[16,2,36864]{2,1,0:T(2,128)(2,1)} %reshape.215), calls=%async_computation | async-start | bytes 4718592 | tf_op jit(solution)/shard_map/all_to_all | solution.py:70
  210.1 2.2 reshape.214
  214.2 2.0 fusion.65
  216.2 1.9 copy.64
  218.1 1.9 copy.63
  220.0 23.2 %all-to-all-done = bf16[16,2,36864]{2,1,0:T(2,128)(2,1)S(1)} async-done(((bf16[16,2,36864]{2,1,0:T(2,128)(2,1)}), bf16[16,2,36864]{2,1,0:T(2,128)(2,1)S(1)}, u32[]{:S(2)}, u32[]{:S(2)}) %all-to-all-start) | async-done | bytes 2359328 | tf_op jit(solution)/shard_map/all_to_all | solution.py:70
  243.1 5.4 %reshape.216 = bf16[16,6,3,64,64]{4,3,2,1,0:T(8,128)(2,1)} reshape(bf16[16,2,36864]{2,1,0:T(2,128)(2,1)S(1)} %all-to-all-done) | data formatting | bytes 4718592
  248.5 6.1 %bitcast_bitcast_fusion = bf16[6,16,64,3,1,64]{5,2,3,0,1,4:T(8,128)(2,1)} fusion(bf16[16,6,3,64,64]{4,3,2,1,0:T(8,128)(2,1)} %reshape.216), kind=kLoop, calls=%fused_computation.92 | loop fusion | bytes 4718592 | tf_op jit(solution)/shard_map/all_to_all | solution.py:70
  254.6 7.3 %copy.44 = bf16[6,16,64,3,1,64]{2,1,5,0,3,4:T(8,128)(2,1)} copy(bf16[6,16,64,3,1,64]{5,2,3,0,1,4:T(8,128)(2,1)} %bitcast_bitcast_fusion) | data formatting | bytes 4718592 | tf_op jit(solution)/shard_map/all_to_all | solution.py:70
  261.9 6.3 %all_to_all.40 = bf16[6,1024,3,1,64]{1,4,0,3,2:T(8,128)(2,1)S(1)} reshape(bf16[6,16,64,3,1,64]{2,1,5,0,3,4:T(8,128)(2,1)} %copy.44) | data formatting | bytes 4718592 | tf_op jit(solution)/shard_map/all_to_all | solution.py:70
  269.1 11.0 %fusion = (f32[6,1024]{1,0:T(8,128)S(1)}, f32[6,1024,1216]{1,2,0:T(8,128)}) fusion(pred[6,1216]{1,0:T(8,128)(4,1)S(1)} %compare_or_fusion, bf16[6,192,64]{1,2,0:T(8,128)(2,1)S(1)} %bitcast.128, bf16[6,1024,64]{1,2,0:T(8,128)(2,1)S(1)} %get-tuple-element.5, bf16[6,1024,3,1,64]{1,4,0,3,2:T(8,128)(2,1)S(1)} %all_to_all.40), kind=kOutput, calls=%fused_computation.2 | convolution fusion | flops 980576256 | bytes 31688704 | tf_op jit(solution)/shard_map/pqhd,pkhd->phqk/dot_general | solution.py:84
  280.1 13.9 %fusion.1 = f32[6,1024]{1,0:T(8,128)S(1)} fusion(f32[6,1024,1216]{1,2,0:T(8,128)} %get-tuple-element.16, f32[6,1024]{1,0:T(8,128)S(1)} %get-tuple-element.15, pred[6,1216]{1,0:T(8,128)(4,1)S(1)} %compare_or_fusion), kind=kLoop, calls=%fused_computation.3 | loop fusion | flops 29878272 | bytes 29940864 | tf_op jit(solution)/shard_map/reduce_sum | solution.py:92
  294.1 13.4 %fusion.24 = bf16[6,1024,1,64]{1,3,0,2:T(8,128)(2,1)} fusion(f32[6,1024,1216]{1,2,0:T(8,128)} %get-tuple-element.16, f32[6,1024]{1,0:T(8,128)S(1)} %get-tuple-element.15, pred[6,1216]{1,0:T(8,128)(4,1)S(1)} %compare_or_fusion, bf16[6,192,64]{1,2,0:T(8,128)(2,1)S(1)} %bitcast.129, bf16[6,1024,64]{1,2,0:T(8,128)(2,1)S(1)} %get-tuple-element.4, ...), kind=kOutput, calls=%fused_computation.26 | convolution fusion | flops 988839936 | bytes 31661184 | tf_op jit(solution)/shard_map/phqk,pkhd->pqhd/dot_general | solution.py:93
  307.5 2.6 copy.51
  310.1 2.2 reshape.217
  312.3 5.2 %all-to-all-start.2 = ((bf16[16,2,12288]{2,1,0:T(2,128)(2,1)}), bf16[16,2,12288]{2,1,0:T(2,128)(2,1)}, u32[]{:S(2)}, u32[]{:S(2)}) async-start(bf16[16,2,12288]{2,1,0:T(2,128)(2,1)} %reshape.217), calls=%async_computation.2 | async-start | bytes 1572864 | tf_op jit(solution)/shard_map/all_to_all | solution.py:101
  317.7 68.7 %all-gather.2 = bf16[128,1,768]{2,1,0:T(2,128)(2,1)S(1)} all-gather(bf16[1,1,768]{2,1,0:T(2,128)(2,1)S(1)} %reshape.202), channel_id=1, replica_groups=mesh['guid'=2,'req'=4,'seq'=16] {'guid','req','seq'}, dimensions={0}, use_global_device_ids=true | all-gather | bytes 198144 | tf_op jit(solution)/shard_map/all_gather | solution.py:54
  388.6 3.5 reshape.218
  392.1 2.2 copy.82
  394.2 2.7 dot_general.27
  397.0 3.4 fusion.68
  403.1 4.8 %collective-permute-done = bf16[6,64,32]{1,2,0:T(8,128)(2,1)S(1)} collective-permute-done((bf16[6,64,32]{1,2,0:T(8,128)(2,1)S(1)}, bf16[6,64,32]{1,2,0:T(8,128)(2,1)S(1)}, u32[]{:S(2)}, u32[]{:S(2)}) %collective-permute-start) | collective-permute-done | bytes 24608 | tf_op jit(solution)/shard_map/ppermute | solution.py:16
  (69 shorter events, 17.8 us)
Async XLA Ops:
  7.2 5.3 %copy-start = (bf16[1,6,64,1536]{3,2,1,0:T(8,128)(2,1)S(1)}, bf16[1,6,64,1536]{3,2,1,0:T(8,128)(2,1)}, u32[]{:S(2)}) copy-start(bf16[1,6,64,1536]{3,2,1,0:T(8,128)(2,1)} %param.11) | copy-start | bytes 3538948
  7.2 5.8 %copy-start.10 = (f32[1,6,2,1536]{3,2,1,0:T(2,128)S(1)}, f32[1,6,2,1536]{3,2,1,0:T(2,128)}, u32[]{:S(2)}) copy-start(f32[1,6,2,1536]{3,2,1,0:T(2,128)} %param.14) | copy-start | bytes 221188
  7.2 5.8 %copy-start.5 = (f32[1,6,5,1536]{3,0,2,1:T(1,128)S(1)}, f32[1,6,5,1536]{3,0,2,1:T(1,128)}, u32[]{:S(2)}) copy-start(f32[1,6,5,1536]{3,0,2,1:T(1,128)} %param.13) | copy-start | bytes 552964
  7.2 79.5 %all-gather.11.cloned.1.call-start = ((), (), s32[]{:S(2)}) async-start(), calls=%async_computation.5 | async-start | bytes 12681216 | tf_op jit(solution)/shard_map/all_gather | solution.py:52
  7.9 154.4 %all-gather.9.cloned.1.call-start = ((), (), s32[]{:S(2)}) async-start(), calls=%async_computation.4 | async-start | bytes 12681216 | tf_op jit(solution)/shard_map/all_gather | solution.py:51
  14.4 86.0 %copy-start.1 = (bf16[1,6,12,1536]{3,2,1,0:T(8,128)(2,1)S(1)}, bf16[1,6,12,1536]{3,2,1,0:T(8,128)(2,1)}, u32[]{:S(2)}) copy-start(bf16[1,6,12,1536]{3,2,1,0:T(8,128)(2,1)} %param.12) | copy-start | bytes 663556
  108.0 94.6 %all-to-all-start.1 = ((bf16[16,2,4608]{2,1,0:T(2,128)(2,1)}), bf16[16,2,4608]{2,1,0:T(2,128)(2,1)}, u32[]{:S(2)}, u32[]{:S(2)}) async-start(bf16[16,2,4608]{2,1,0:T(2,128)(2,1)} %reshape.213), calls=%async_computation.1 | async-start | bytes 589824 | tf_op jit(solution)/shard_map/all_to_all | solution.py:72
  202.6 7.4 %copy-start.12 = (s32[1,6]{1,0:T(1,128)S(1)}, s32[1,6]{1,0:T(1,128)}, u32[]{:S(2)}) copy-start(s32[1,6]{1,0:T(1,128)} %param.19) | copy-start | bytes 76
  202.6 40.5 %all-to-all-start = ((bf16[16,2,36864]{2,1,0:T(2,128)(2,1)}), bf16[16,2,36864]{2,1,0:T(2,128)(2,1)S(1)}, u32[]{:S(2)}, u32[]{:S(2)}) async-start(bf16[16,2,36864]{2,1,0:T(2,128)(2,1)} %reshape.215), calls=%async_computation | async-start | bytes 4718592 | tf_op jit(solution)/shard_map/all_to_all | solution.py:70
  209.3 187.7 %all-gather.7.cloned.1.call-start = ((), (), s32[]{:S(2)}) async-start(), calls=%async_computation.3 | async-start | bytes 3170304 | tf_op jit(solution)/shard_map/all_gather | solution.py:57
  268.2 0.9 copy-start.2
  280.1 14.0 %copy-start.4 = (bf16[6,192,1,1,64]{1,4,0,3,2:T(8,128)(2,1)S(1)}, bf16[6,192,1,1,64]{1,4,0,3,2:T(8,128)(2,1)}, u32[]{:S(2)}) copy-start(bf16[6,192,1,1,64]{1,4,0,3,2:T(8,128)(2,1)} %copy.63) | copy-start | bytes 442372
  310.1 7.5 %copy-start.8 = (f32[1,6,1,1536]{3,0,2,1:T(1,128)S(1)}, f32[1,6,1,1536]{3,0,2,1:T(1,128)}, u32[]{:S(2)}) copy-start(f32[1,6,1,1536]{3,0,2,1:T(1,128)} %get-tuple-element.10) | copy-start | bytes 110596
  310.1 7.5 %copy-start.11 = (bf16[12,64]{1,0:T(8,128)(2,1)S(1)}, bf16[12,64]{1,0:T(8,128)(2,1)}, u32[]{:S(2)}) copy-start(bf16[12,64]{1,0:T(8,128)(2,1)} %param.18) | copy-start | bytes 4612
  310.1 78.5 %copy-start.6 = (f32[1,6,1,1536]{3,0,2,1:T(1,128)S(1)}, f32[1,6,1,1536]{3,0,2,1:T(1,128)}, u32[]{:S(2)}) copy-start(f32[1,6,1,1536]{3,0,2,1:T(1,128)} %get-tuple-element.8) | copy-start | bytes 110596
  310.1 78.5 %copy-start.7 = (f32[1,6,1,1536]{3,0,2,1:T(1,128)S(1)}, f32[1,6,1,1536]{3,0,2,1:T(1,128)}, u32[]{:S(2)}) copy-start(f32[1,6,1,1536]{3,0,2,1:T(1,128)} %get-tuple-element.11) | copy-start | bytes 110596
  312.3 76.3 %all-to-all-start.2 = ((bf16[16,2,12288]{2,1,0:T(2,128)(2,1)}), bf16[16,2,12288]{2,1,0:T(2,128)(2,1)}, u32[]{:S(2)}, u32[]{:S(2)}) async-start(bf16[16,2,12288]{2,1,0:T(2,128)(2,1)} %reshape.217), calls=%async_computation.2 | async-start | bytes 1572864 | tf_op jit(solution)/shard_map/all_to_all | solution.py:101
  400.4 1.0 copy-start.3
  400.4 7.6 %copy-start.9 = (f32[6,64,32]{1,2,0:T(8,128)S(1)}, f32[6,64,32]{1,2,0:T(8,128)}, u32[]{:S(2)}) copy-start(f32[6,64,32]{1,2,0:T(8,128)} %param.20) | copy-start | bytes 147460
  402.3 5.7 %collective-permute-start = (bf16[6,64,32]{1,2,0:T(8,128)(2,1)S(1)}, bf16[6,64,32]{1,2,0:T(8,128)(2,1)S(1)}, u32[]{:S(2)}, u32[]{:S(2)}) collective-permute-start(bf16[6,64,32]{1,2,0:T(8,128)(2,1)S(1)} %dynamic-slice_convert_fusion), channel_id=1, source_target_pairs={{0,64},{64,0},{1,65},{65,1},{2,66},{66,2},{3,67},{67,3},{4,68},{68... | collective-permute-start | bytes 73736 | tf_op jit(solution)/shard_map/ppermute | solution.py:16
Sparse Core Ops, SparseCore 0:
  11.1 75.5 all-gather.10
  89.7 72.5 all-gather.8
  213.2 73.6 all-gather.6
where the time goes:
time: 417 us; the launch traced here: 415 us
  waiting for transfers between devices  150 us (36%)
  local copies, waits for them, and re-layouts  99.3 us (24%)
  blocking collectives  68.7 us (16%)
  matrix products  42.3 us (10%)
  other arithmetic  21.2 us (5%)
  starting transfers between devices  18.9 us (5%)
  between operations  14.9 us (4%)
    all_gather x1, waiting for transfers between devices, local(): full_txt = lax.all_gather(w_txt_qkv, all_axes, axis=0, tiled=True)  72.3 us
    all_gather x1, blocking collectives, local(): lax.all_gather(w_head.reshape(1, head_rows * head_cols), all_axes, axis=0...  68.7 us
    unnamed x38, local copies, waits for them, and re-layouts  54.8 us
    all_gather x1, waiting for transfers between devices, local(): full_img = lax.all_gather(w_img_qkv, all_axes, axis=0, tiled=True)  47.7 us
    all_to_all x1, waiting for transfers between devices, local(): img_heads = lax.all_to_all(img_split, 'seq', 3, 1, tiled=True)  23.2 us
    all_to_all x3, local copies, waits for them, and re-layouts, local(): img_heads = lax.all_to_all(img_split, 'seq', 3, 1, tiled=True)  19.7 us
    reduce_sum x1, other arithmetic, local(): totals = jnp.sum(weights, axis=-1)  13.9 us
    dot_general x1, matrix products, local(): jnp.einsum('phqk,pkhd->pqhd', weights.astype(jnp.bfloat16), value_heads,...  13.4 us
  transfers between devices with their start and end apart: 7, of which 4 were waited for; matrix products, arithmetic and copies ran while one was open for 36% of the time, Pallas kernels for 0%

commit v1 on v0

--- a/solution.py
+++ b/solution.py
@@ -49,7 +49,16 @@
     model_width = img_hidden.shape[3]
     nseq = lax.axis_size("seq")
     full_img = lax.all_gather(w_img_qkv, all_axes, axis=0, tiled=True)
-    full_txt = lax.all_gather(w_txt_qkv, all_axes, axis=0, tiled=True)
+
+    def watch_roots_for(local_block, ndim_at):
+        return jnp.concatenate(
+            lax.all_to_all(
+                jnp.stack([local_block for _ in range(lax.axis_size(all_axes))]), all_axes, 0, 0
+            ),
+            axis=ndim_at,
+        )
+
+    full_txt = watch_roots_for(w_txt_qkv, ndim_at=0)
     head_rows, head_cols = w_head.shape
     full_head = lax.all_gather(
         w_head.reshape(1, head_rows * head_cols), all_axes, axis=0, tiled=True

time: 417 us -> 480 us (1.15)
  waiting for transfers between devices: 150 us -> 187 us
  starting transfers between devices: 18.9 us -> 33.5 us
  local copies, waits for them, and re-layouts: 99.3 us -> 107 us
  blocking collectives: 68.7 us -> 74.6 us
    all_to_all x0 -> x1, waiting for transfers between devices: none -> 160 us  [watch_roots_for(): lax.all_to_all(jnp.stack([local_block for _ in range(lax.axis_size(all_ax...]
    all_gather x1 -> x0, waiting for transfers between devices: 72.3 us -> none  [local(): full_txt = lax.all_gather(w_txt_qkv, all_axes, axis=0, tiled=True)]
    all_gather x1, waiting for transfers between devices: 47.7 us -> 0.02 us  [local(): full_img = lax.all_gather(w_img_qkv, all_axes, axis=0, tiled=True)]
    reshape x0 -> x1, local copies, waits for them, and re-layouts: none -> 14.4 us  [watch_roots_for(): jnp.concatenate(lax.all_to_all(jnp.stack([local_block for _ in range(lax....]
    unnamed x38 -> x37, local copies, waits for them, and re-layouts: 54.8 us -> 41.1 us
    all_to_all x0 -> x1, starting transfers between devices: none -> 11.6 us  [watch_roots_for(): lax.all_to_all(jnp.stack([local_block for _ in range(lax.axis_size(all_ax...]
    another operation x0 -> x1, local copies, waits for them, and re-layouts: none -> 7.09 us  [watch_roots_for(): jnp.stack([local_block for _ in range(lax.axis_size(all_axes))])]
    all_gather x1, blocking collectives: 68.7 us -> 74.6 us  [local(): lax.all_gather(w_head.reshape(1, head_rows * head_cols), all_axes, axis=0...]
  transfers between devices with their start and end apart: 7 -> 7, of which waited for: 4 -> 3; matrix products, arithmetic and copies ran while one was open for 36% -> 32% of each run, Pallas kernels for 0% -> 0%
where the time goes in v1:
time: 480 us; the launch traced here: 478 us
  waiting for transfers between devices  187 us (39%)
  local copies, waits for them, and re-layouts  107 us (22%)
  blocking collectives  74.6 us (16%)
  matrix products  42.6 us (9%)
  starting transfers between devices  33.5 us (7%)
  other arithmetic  18.1 us (4%)
  between operations  15.2 us (3%)
    all_to_all x1, waiting for transfers between devices, watch_roots_for(): lax.all_to_all(jnp.stack([local_block for _ in range(lax.axis_size(all_ax...  160 us
    all_gather x1, blocking collectives, local(): lax.all_gather(w_head.reshape(1, head_rows * head_cols), all_axes, axis=0...  74.6 us
    unnamed x37, local copies, waits for them, and re-layouts  41.1 us
    all_to_all x1, waiting for transfers between devices, local(): img_heads = lax.all_to_all(img_split, 'seq', 3, 1, tiled=True)  20.5 us
    all_to_all x3, local copies, waits for them, and re-layouts, local(): img_heads = lax.all_to_all(img_split, 'seq', 3, 1, tiled=True)  19.7 us
    reshape x1, local copies, waits for them, and re-layouts, watch_roots_for(): jnp.concatenate(lax.all_to_all(jnp.stack([local_block for _ in range(lax....  14.4 us
    reduce_sum x1, other arithmetic, local(): totals = jnp.sum(weights, axis=-1)  14 us
    dot_general x1, matrix products, local(): jnp.einsum('phqk,pkhd->pqhd', weights.astype(jnp.bfloat16), value_heads,...  13.4 us
  transfers between devices with their start and end apart: 7, of which 3 were waited for; matrix products, arithmetic and copies ran while one was open for 32% of the time, Pallas kernels for 0%

profile of v1, /device:TPU:0, one launch (start us, length us, event | category | flops | bytes accessed | tf_op | source)
XLA Modules:
  0.0 477.9 jit_solution(2232887923609762981)
XLA Ops:
  7.9 7.1 %stack.2 = bf16[128,12,3072]{2,1,0:T(8,128)(2,1)} broadcast(bf16[12,3072]{1,0:T(8,128)(2,1)} %param.16), dimensions={1,2} | broadcast | bytes 9510912 | tf_op jit(solution)/shard_map/stack | solution.py:56
  15.0 11.6 %all-to-all-start.1 = ((bf16[128,12,3072]{2,1,0:T(8,128)(2,1)}), bf16[128,12,3072]{2,1,0:T(8,128)(2,1)}, u32[]{:S(2)}, u32[]{:S(2)}) async-start(bf16[128,12,3072]{2,1,0:T(8,128)(2,1)} %stack.2), calls=%async_computation.1 | async-start | bytes 25165824 | tf_op jit(solution)/shard_map/all_to_all | solution.py:55
  29.1 160.3 %all-to-all-done.1 = bf16[128,12,3072]{2,1,0:T(8,128)(2,1)} async-done(((bf16[128,12,3072]{2,1,0:T(8,128)(2,1)}), bf16[128,12,3072]{2,1,0:T(8,128)(2,1)}, u32[]{:S(2)}, u32[]{:S(2)}) %all-to-all-start.1) | async-done | bytes 9437216 | tf_op jit(solution)/shard_map/all_to_all | solution.py:55
  189.4 14.4 %reshape.212 = bf16[1536,3072,1]{1,0,2:T(8,128)(2,1)} reshape(bf16[128,12,3072]{2,1,0:T(8,128)(2,1)} %all-to-all-done.1) | data formatting | bytes 18874368 | tf_op jit(solution)/shard_map/reshape | solution.py:54
  203.8 5.7 %fusion.49 = bf16[6,12,3072]{2,1,0:T(8,128)(2,1)S(1)} fusion(bf16[1536,3072,1]{1,0,2:T(8,128)(2,1)} %reshape.212, bf16[1,6,12,1536]{3,2,1,0:T(8,128)(2,1)S(1)} %copy-done.1, f32[6,1536]{1,0:T(8,128)S(1)} %get-tuple-element.19, f32[6,1536]{1,0:T(8,128)S(1)} %get-tuple-element.20, f32[6,12]{1,0:T(8,128)S(1)} %add_rsqrt_fusion.1, ...), kind=kOutput, calls=%fused_computation.55 | convolution fusion | flops 680140800 | bytes 10175040 | tf_op jit(solution)/shard_map/prd,de->pre/dot_general | solution.py:75
  211.7 9.9 %all-to-all-start.2 = ((bf16[16,2,4608]{2,1,0:T(2,128)(2,1)}), bf16[16,2,4608]{2,1,0:T(2,128)(2,1)}, u32[]{:S(2)}, u32[]{:S(2)}) async-start(bf16[16,2,4608]{2,1,0:T(2,128)(2,1)} %reshape.218), calls=%async_computation.2 | async-start | bytes 589824 | tf_op jit(solution)/shard_map/all_to_all | solution.py:81
  221.7 13.7 %reshape.211 = bf16[1536,3072,1]{1,0,2:T(8,128)(2,1)} reshape(bf16[128,12,3072]{2,1,0:T(8,128)(2,1)} %all-gather.7.cloned.1.call-done) | data formatting | bytes 18874368
  235.4 8.2 %convolution_convert_fusion = bf16[6,64,3072]{2,1,0:T(8,128)(2,1)S(1)} fusion(bf16[1536,3072,1]{1,0,2:T(8,128)(2,1)} %reshape.211, bf16[1,6,64,1536]{3,2,1,0:T(8,128)(2,1)S(1)} %copy-done, f32[6,1536]{1,0:T(8,128)} %get-tuple-element.24, f32[6,1536]{1,0:T(8,128)} %get-tuple-element.23, f32[6,64]{1,0:T(8,128)S(1)} %add_rsqrt_fusion.2, ...), kind=kOutput, calls=%fused_computation.7 | convolution fusion | flops 3628597248 | bytes 13052928 | tf_op jit(solution)/shard_map/prd,de->pre/dot_general | solution.py:72
  243.6 4.8 %reshape.188 = bf16[6,64,3,16,64]{4,3,2,1,0:T(8,128)(2,1)} reshape(bf16[6,64,3072]{2,1,0:T(8,128)(2,1)S(1)} %convolution_convert_fusion) | data formatting | bytes 4718592 | tf_op jit(solution)/shard_map/reshape | solution.py:78
  248.4 5.8 %copy.84 = bf16[6,64,3,16,64]{4,1,2,0,3:T(8,128)(2,1)} copy(bf16[6,64,3,16,64]{4,3,2,1,0:T(8,128)(2,1)} %reshape.188) | data formatting | bytes 4718592 | tf_op jit(solution)/shard_map/reshape | solution.py:78
  254.2 7.8 %reshape.220 = bf16[16,2,36864]{2,1,0:T(2,128)(2,1)} reshape(bf16[16,6,3,64,64]{4,3,2,1,0:T(8,128)(2,1)} %bitcast.115) | data formatting | bytes 4718592
  262.0 7.3 %all-to-all-start = ((bf16[16,2,36864]{2,1,0:T(2,128)(2,1)}), bf16[16,2,36864]{2,1,0:T(2,128)(2,1)S(1)}, u32[]{:S(2)}, u32[]{:S(2)}) async-start(bf16[16,2,36864]{2,1,0:T(2,128)(2,1)} %reshape.220), calls=%async_computation | async-start | bytes 4718592 | tf_op jit(solution)/shard_map/all_to_all | solution.py:79
  270.2 2.2 reshape.219
  274.3 2.0 fusion.66
  276.3 1.9 copy.64
  280.1 20.5 %all-to-all-done = bf16[16,2,36864]{2,1,0:T(2,128)(2,1)S(1)} async-done(((bf16[16,2,36864]{2,1,0:T(2,128)(2,1)}), bf16[16,2,36864]{2,1,0:T(2,128)(2,1)S(1)}, u32[]{:S(2)}, u32[]{:S(2)}) %all-to-all-start) | async-done | bytes 2359328 | tf_op jit(solution)/shard_map/all_to_all | solution.py:79
  300.6 5.3 %reshape.221 = bf16[16,6,3,64,64]{4,3,2,1,0:T(8,128)(2,1)} reshape(bf16[16,2,36864]{2,1,0:T(2,128)(2,1)S(1)} %all-to-all-done) | data formatting | bytes 4718592
  305.9 6.1 %bitcast_bitcast_fusion = bf16[6,16,64,3,1,64]{5,2,3,0,1,4:T(8,128)(2,1)} fusion(bf16[16,6,3,64,64]{4,3,2,1,0:T(8,128)(2,1)} %reshape.221), kind=kLoop, calls=%fused_computation.94 | loop fusion | bytes 4718592 | tf_op jit(solution)/shard_map/all_to_all | solution.py:79
  312.0 7.3 %copy.44 = bf16[6,16,64,3,1,64]{2,1,5,0,3,4:T(8,128)(2,1)} copy(bf16[6,16,64,3,1,64]{5,2,3,0,1,4:T(8,128)(2,1)} %bitcast_bitcast_fusion) | data formatting | bytes 4718592 | tf_op jit(solution)/shard_map/all_to_all | solution.py:79
  319.3 6.3 %all_to_all.43 = bf16[6,1024,3,1,64]{1,4,0,3,2:T(8,128)(2,1)S(1)} reshape(bf16[6,16,64,3,1,64]{2,1,5,0,3,4:T(8,128)(2,1)} %copy.44) | data formatting | bytes 4718592 | tf_op jit(solution)/shard_map/all_to_all | solution.py:79
  326.6 11.0 %fusion = (f32[6,1024]{1,0:T(8,128)S(1)}, f32[6,1024,1216]{1,2,0:T(8,128)}) fusion(pred[6,1216]{1,0:T(8,128)(4,1)S(1)} %compare_or_fusion, bf16[6,192,64]{1,2,0:T(8,128)(2,1)S(1)} %bitcast.121, bf16[6,1024,64]{1,2,0:T(8,128)(2,1)S(1)} %get-tuple-element.5, bf16[6,1024,3,1,64]{1,4,0,3,2:T(8,128)(2,1)S(1)} %all_to_all.43), kind=kOutput, calls=%fused_computation.2 | convolution fusion | flops 980576256 | bytes 31688704 | tf_op jit(solution)/shard_map/pqhd,pkhd->phqk/dot_general | solution.py:93
  337.6 14.0 %fusion.1 = f32[6,1024]{1,0:T(8,128)S(1)} fusion(f32[6,1024,1216]{1,2,0:T(8,128)} %get-tuple-element.16, f32[6,1024]{1,0:T(8,128)S(1)} %get-tuple-element.15, pred[6,1216]{1,0:T(8,128)(4,1)S(1)} %compare_or_fusion), kind=kLoop, calls=%fused_computation.3 | loop fusion | flops 29878272 | bytes 29940864 | tf_op jit(solution)/shard_map/reduce_sum | solution.py:101
  351.6 13.4 %fusion.24 = bf16[6,1024,1,64]{1,3,0,2:T(8,128)(2,1)} fusion(f32[6,1024,1216]{1,2,0:T(8,128)} %get-tuple-element.16, f32[6,1024]{1,0:T(8,128)S(1)} %get-tuple-element.15, pred[6,1216]{1,0:T(8,128)(4,1)S(1)} %compare_or_fusion, bf16[6,192,64]{1,2,0:T(8,128)(2,1)S(1)} %bitcast.122, bf16[6,1024,64]{1,2,0:T(8,128)(2,1)S(1)} %get-tuple-element.4, ...), kind=kOutput, calls=%fused_computation.26 | convolution fusion | flops 988839936 | bytes 31661184 | tf_op jit(solution)/shard_map/phqk,pkhd->pqhd/dot_general | solution.py:102
  365.0 2.6 copy.51
  367.7 2.2 reshape.222
  369.9 4.3 all-to-all-start.3
  374.3 74.6 %all-gather.1 = bf16[128,1,768]{2,1,0:T(2,128)(2,1)S(1)} all-gather(bf16[1,1,768]{2,1,0:T(2,128)(2,1)S(1)} %reshape.207), channel_id=1, replica_groups=mesh['guid'=2,'req'=4,'seq'=16] {'guid','req','seq'}, dimensions={0}, use_global_device_ids=true | all-gather | bytes 198144 | tf_op jit(solution)/shard_map/all_gather | solution.py:63
  451.1 3.5 reshape.223
  454.5 2.2 copy.82
  456.7 2.7 dot_general.27
  459.4 3.4 fusion.69
  465.6 4.8 %collective-permute-done = bf16[6,64,32]{1,2,0:T(8,128)(2,1)S(1)} collective-permute-done((bf16[6,64,32]{1,2,0:T(8,128)(2,1)S(1)}, bf16[6,64,32]{1,2,0:T(8,128)(2,1)S(1)}, u32[]{:S(2)}, u32[]{:S(2)}) %collective-permute-start) | collective-permute-done | bytes 24608 | tf_op jit(solution)/shard_map/ppermute | solution.py:16
  (69 shorter events, 15.8 us)
Async XLA Ops:
  7.2 214.5 %all-gather.7.cloned.1.call-start = ((), (), s32[]{:S(2)}) async-start(), calls=%async_computation.5 | async-start | bytes 12681216 | tf_op jit(solution)/shard_map/all_gather | solution.py:51
  15.0 11.7 %copy-start.1 = (bf16[1,6,12,1536]{3,2,1,0:T(8,128)(2,1)S(1)}, bf16[1,6,12,1536]{3,2,1,0:T(8,128)(2,1)}, u32[]{:S(2)}) copy-start(bf16[1,6,12,1536]{3,2,1,0:T(8,128)(2,1)} %param.12) | copy-start | bytes 663556
  15.0 12.0 %copy-start = (bf16[1,6,64,1536]{3,2,1,0:T(8,128)(2,1)S(1)}, bf16[1,6,64,1536]{3,2,1,0:T(8,128)(2,1)}, u32[]{:S(2)}) copy-start(bf16[1,6,64,1536]{3,2,1,0:T(8,128)(2,1)} %param.11) | copy-start | bytes 3538948
  15.0 174.4 %all-to-all-start.1 = ((bf16[128,12,3072]{2,1,0:T(8,128)(2,1)}), bf16[128,12,3072]{2,1,0:T(8,128)(2,1)}, u32[]{:S(2)}, u32[]{:S(2)}) async-start(bf16[128,12,3072]{2,1,0:T(8,128)(2,1)} %stack.2), calls=%async_computation.1 | async-start | bytes 25165824 | tf_op jit(solution)/shard_map/all_to_all | solution.py:55
  26.6 1.1 copy-start.10
  26.7 1.2 copy-start.5
  211.7 50.3 %all-to-all-start.2 = ((bf16[16,2,4608]{2,1,0:T(2,128)(2,1)}), bf16[16,2,4608]{2,1,0:T(2,128)(2,1)}, u32[]{:S(2)}, u32[]{:S(2)}) async-start(bf16[16,2,4608]{2,1,0:T(2,128)(2,1)} %reshape.218), calls=%async_computation.2 | async-start | bytes 589824 | tf_op jit(solution)/shard_map/all_to_all | solution.py:81
  262.0 8.1 %copy-start.12 = (s32[1,6]{1,0:T(1,128)S(1)}, s32[1,6]{1,0:T(1,128)}, u32[]{:S(2)}) copy-start(s32[1,6]{1,0:T(1,128)} %param.19) | copy-start | bytes 76
  262.0 38.5 %all-to-all-start = ((bf16[16,2,36864]{2,1,0:T(2,128)(2,1)}), bf16[16,2,36864]{2,1,0:T(2,128)(2,1)S(1)}, u32[]{:S(2)}, u32[]{:S(2)}) async-start(bf16[16,2,36864]{2,1,0:T(2,128)(2,1)} %reshape.220), calls=%async_computation | async-start | bytes 4718592 | tf_op jit(solution)/shard_map/all_to_all | solution.py:79
  269.3 190.1 %all-gather.5.cloned.1.call-start = ((), (), s32[]{:S(2)}) async-start(), calls=%async_computation.4 | async-start | bytes 3170304 | tf_op jit(solution)/shard_map/all_gather | solution.py:66
  325.6 0.9 copy-start.2
  337.6 14.0 %copy-start.4 = (bf16[6,192,1,1,64]{1,4,0,3,2:T(8,128)(2,1)S(1)}, bf16[6,192,1,1,64]{1,4,0,3,2:T(8,128)(2,1)}, u32[]{:S(2)}) copy-start(bf16[6,192,1,1,64]{1,4,0,3,2:T(8,128)(2,1)} %copy.63) | copy-start | bytes 442372
  367.6 6.5 %copy-start.8 = (f32[1,6,1,1536]{3,0,2,1:T(1,128)S(1)}, f32[1,6,1,1536]{3,0,2,1:T(1,128)}, u32[]{:S(2)}) copy-start(f32[1,6,1,1536]{3,0,2,1:T(1,128)} %get-tuple-element.10) | copy-start | bytes 110596
  367.6 6.6 %copy-start.11 = (bf16[12,64]{1,0:T(8,128)(2,1)S(1)}, bf16[12,64]{1,0:T(8,128)(2,1)}, u32[]{:S(2)}) copy-start(bf16[12,64]{1,0:T(8,128)(2,1)} %param.18) | copy-start | bytes 4612
  367.7 83.4 %copy-start.6 = (f32[1,6,1,1536]{3,0,2,1:T(1,128)S(1)}, f32[1,6,1,1536]{3,0,2,1:T(1,128)}, u32[]{:S(2)}) copy-start(f32[1,6,1,1536]{3,0,2,1:T(1,128)} %get-tuple-element.8) | copy-start | bytes 110596
  367.7 83.4 %copy-start.7 = (f32[1,6,1,1536]{3,0,2,1:T(1,128)S(1)}, f32[1,6,1,1536]{3,0,2,1:T(1,128)}, u32[]{:S(2)}) copy-start(f32[1,6,1,1536]{3,0,2,1:T(1,128)} %get-tuple-element.11) | copy-start | bytes 110596
  369.9 81.2 %all-to-all-start.3 = ((bf16[16,2,12288]{2,1,0:T(2,128)(2,1)}), bf16[16,2,12288]{2,1,0:T(2,128)(2,1)}, u32[]{:S(2)}, u32[]{:S(2)}) async-start(bf16[16,2,12288]{2,1,0:T(2,128)(2,1)} %reshape.222), calls=%async_computation.3 | async-start | bytes 1572864 | tf_op jit(solution)/shard_map/all_to_all | solution.py:110
  462.8 1.0 copy-start.3
  462.8 7.6 %copy-start.9 = (f32[6,64,32]{1,2,0:T(8,128)S(1)}, f32[6,64,32]{1,2,0:T(8,128)}, u32[]{:S(2)}) copy-start(f32[6,64,32]{1,2,0:T(8,128)} %param.20) | copy-start | bytes 147460
  464.7 5.7 %collective-permute-start = (bf16[6,64,32]{1,2,0:T(8,128)(2,1)S(1)}, bf16[6,64,32]{1,2,0:T(8,128)(2,1)S(1)}, u32[]{:S(2)}, u32[]{:S(2)}) collective-permute-start(bf16[6,64,32]{1,2,0:T(8,128)(2,1)S(1)} %dynamic-slice_convert_fusion), channel_id=1, source_target_pairs={{0,64},{64,0},{1,65},{65,1},{2,66},{66,2},{3,67},{67,3},{4,68},{68... | collective-permute-start | bytes 73736 | tf_op jit(solution)/shard_map/ppermute | solution.py:16
Sparse Core Ops, SparseCore 0:
  11.1 203.8 all-gather.6
  273.2 79.1 all-gather.4
